TPU v7x, 32 devices: a whole 2x2x4 slice. The times are simulated.
32 devices in a mesh: owner: 2 (over x), reader: 16 (over z, y, core).
Axes of the slice: x: 2, y: 2, z: 4, core: 2. Of those that a mesh axis runs over, the one named last changes fastest.
Arguments:
- acts: bfloat16 [256, 4096], P('reader', 'owner'), may hold values from -6 to 6
- grads: bfloat16 [256, 14336], P('reader', 'owner'), may hold values from -6 to 6
- basis_a: bfloat16 [4096, 4096], P('reader', 'owner'), may hold values from -0.09375 to 0.09375
- basis_g: bfloat16 [14336, 14336], P('reader', 'owner'), may hold values from -0.046875 to 0.046875
- eigvals: bfloat16 [14336, 4096], P('reader', 'owner'), may hold values from 0.099609375 to 10
- lengths: int32 [2], replicated, may hold values from 1 to 128, as said below
- shuffle: int32 [2], replicated, may hold values from 0 to 1, each once
Outputs:
- token_score: float32 [256], P('owner')
- example_score: float32 [2], replicated
Inputs may be any that keep to these rules, and one draw needn't show every extreme that they name: `lengths`: some slot has exactly 128 live tokens. `shuffle`: each example id appears once.
All inputs are finite; a program needn't handle non-finite values.
Results may differ from a plain program's by a relative error of at most 0.0003.
Values may be sent and summed in bfloat16 or wider, within the bound.
No kernel may reach another device: no remote copies, remote signals or barrier semaphores. Data moves between devices by JAX's collectives and lax.ppermute only.
A program may use at most 128 MiB of HBM per device.

v0:
```python
import jax
import jax.numpy as jnp
from jax import lax
from jax.sharding import PartitionSpec as P

SEQ = 128


def local(acts, grads, basis_a, basis_g, eigvals, lengths, shuffle):
    owners = lax.axis_size("owner")
    readers = lax.axis_size("reader")
    owner_index = lax.axis_index("owner")
    rows = acts.shape[0] * readers
    slots = rows // SEQ
    m_block = basis_g.shape[0]
    n_block = basis_a.shape[0]
    width = eigvals.shape[1]
    dim_ff = m_block * readers
    dim_d = width * owners
    joined = jnp.concatenate([grads, acts], axis=1)
    joined = lax.all_gather(joined, "reader", axis=0, tiled=True)
    all_g = joined[:, : grads.shape[1]]
    all_a = joined[:, grads.shape[1] :]
    part_g = jnp.einsum("tk,jk->tj", all_g, basis_g, preferred_element_type=jnp.float32)
    part_a = jnp.einsum("tk,jk->tj", all_a, basis_a, preferred_element_type=jnp.float32)
    part = jnp.concatenate([part_g, part_a], axis=1)
    whole = lax.psum(part, "owner")
    token = jnp.arange(rows, dtype=jnp.int32)
    live = (token % SEQ < lengths[token // SEQ]).astype(jnp.float32)
    rot = (whole * live[:, None]).astype(jnp.bfloat16)
    rot_g = rot[:, :m_block]
    rot_a_block = rot[:, m_block:]
    rot_a_all = lax.all_gather(rot_a_block, "reader", axis=1, tiled=True)
    rot_a = lax.dynamic_slice_in_dim(rot_a_all, owner_index * width, width, axis=1)
    denom = eigvals.astype(jnp.float32)
    g_rows = rot_g.reshape(slots, SEQ, m_block)
    a_rows = rot_a.reshape(slots, SEQ, width)
    outer = jnp.einsum("smt,smn->stn", g_rows, a_rows, preferred_element_type=jnp.float32)
    scaled = (outer / denom[None]).astype(jnp.bfloat16)
    projected = jnp.einsum("stm,smn->stn", g_rows, scaled, preferred_element_type=jnp.float32)
    partial = jnp.sum(projected * a_rows.astype(jnp.float32), axis=2) / (dim_ff * dim_d)
    scores = lax.psum(partial, ("owner", "reader"))
    token_score = lax.dynamic_index_in_dim(scores, owner_index, 0, keepdims=False)
    slot_mean = jnp.sum(scores, axis=1) / SEQ
    table = (shuffle[:, None] == jnp.arange(slots, dtype=jnp.int32)[None, :]).astype(jnp.float32)
    example_score = jnp.sum(slot_mean[:, None] * table, axis=0)
    return (token_score, example_score)


def solution(mesh):
    return jax.shard_map(
        local,
        mesh=mesh,
        in_specs=(
            P("reader", "owner"),
            P("reader", "owner"),
            P("reader", "owner"),
            P("reader", "owner"),
            P("reader", "owner"),
            P(),
            P(),
        ),
        out_specs=(P("owner"), P()),
        check_vma=False,
    )
```

profile of v0, /device:TPU:0, one launch (start us, length us, event | category | flops | bytes accessed | tf_op | source)
XLA Modules:
  0.0 220.0 jit_solution(6955430692185103928)
XLA Ops:
  7.2 0.0 copy-start
  7.2 0.0 all-gather.3.cloned.1.call-start
  7.2 1.8 pad_maximum_fusion.1
  9.0 0.0 all-gather.3.cloned.1.call-update
  9.0 0.0 all-reduce.2.cloned.1.call-start
  9.1 57.3 %all-gather.3.cloned.1.call-done = bf16[256,9216]{1,0:T(8,128)(2,1)} async-done(((bf16[16,9216]{1,0:T(8,128)(2,1)}), bf16[256,9216]{1,0:T(8,128)(2,1)}) %all-gather.3.cloned.1.call-update) | async-done | bytes 4718608 | tf_op jit(solution)/shard_map/all_gather | solution.py:21
  66.4 0.0 copy-done
  66.4 1.7 fusion.7
  68.1 0.0 copy-start.1
  68.1 10.2 %fusion.3 = f32[256,896]{1,0:T(8,128)S(1)} fusion(bf16[896,7168]{1,0:T(8,128)(2,1)} %param.10, bf16[256,9216]{1,0:T(8,128)(2,1)} %all-gather.3.cloned.1.call-done), kind=kOutput, calls=%fused_computation.3 | convolution fusion | flops 3288334336 | bytes 17432576 | tf_op jit(solution)/shard_map/tk,jk->tj/dot_general | solution.py:24
  78.4 1.1 pad_maximum_fusion
  79.5 0.0 all-reduce.2.cloned.1.call-update
  79.5 0.0 all-gather.5.cloned.1.call-start
  79.6 0.0 copy-done.1
  79.6 0.6 fusion.10
  80.2 1.3 compare_select_fusion.1
  81.5 39.7 %all-reduce.2.cloned.1.call-done = f32[256,1152]{1,0:T(8,128)} async-done(((f32[256,1152]{1,0:T(8,128)}), f32[256,1152]{1,0:T(8,128)}) %all-reduce.2.cloned.1.call-update) | async-done | bytes 1179664 | tf_op jit(solution)/shard_map/psum | solution.py:27
  121.2 1.4 multiply_convert_fusion
  122.6 0.7 slice.22
  123.2 0.0 all-gather.5.cloned.1.call-update
  123.3 5.9 %convert_element_type.22 = f32[896,2048]{1,0:T(8,128)} convert(bf16[896,2048]{1,0:T(8,128)(2,1)} %param.11) | non-fusion elementwise | flops 1835008 | bytes 11010048 | tf_op jit(solution)/shard_map/convert_element_type | solution.py:35
  129.2 35.5 %all-gather.5.cloned.1.call-done = bf16[256,4096]{1,0:T(8,128)(2,1)} async-done(((bf16[256,256]{1,0:T(8,128)(2,1)}), bf16[256,4096]{1,0:T(8,128)(2,1)}) %all-gather.5.cloned.1.call-update) | async-done | bytes 2097168 | tf_op jit(solution)/shard_map/all_gather | solution.py:33
  164.8 1.3 constant_dynamic-slice_fusion
  166.1 0.0 copy-start.2
  166.1 6.4 %fusion.6 = f32[2,128]{1,0:T(2,128)S(1)} fusion(bf16[2,128,2048]{2,1,0:T(8,128)(2,1)S(1)} %bitcast.12, bf16[2,128,896]{2,1,0:T(8,128)(2,1)S(1)} %bitcast.13, f32[896,2048]{1,0:T(8,128)} %convert_element_type.22), kind=kOutput, calls=%fused_computation.6 | convolution fusion | flops 1887960832 | bytes 8848384 | tf_op jit(solution)/shard_map/stm,smn->stn/dot_general | solution.py:40
  172.5 39.7 %psum.15 = f32[2,128]{1,0:T(2,128)S(1)} all-reduce(f32[2,128]{1,0:T(2,128)S(1)} %broadcast_multiply_fusion), channel_id=1, replica_groups=mesh['owner'=2,'reader'=16] {'owner','reader'}, use_global_device_ids=true, to_apply=%region_2.3 | all-reduce | flops 256 | bytes 2048 | tf_op jit(solution)/shard_map/psum | solution.py:42
  212.2 0.5 dynamic-slice_bitcast_fusion
  212.7 0.1 reduce_sum.28
  212.9 0.0 copy-done.2
  212.9 0.6 fusion.9
  (4 shorter events, 0.1 us)
Async XLA Ops:
  7.2 59.3 %copy-start = (bf16[256,2048]{1,0:T(8,128)(2,1)S(1)}, bf16[256,2048]{1,0:T(8,128)(2,1)}, u32[]{:S(2)}) copy-start(bf16[256,2048]{1,0:T(8,128)(2,1)} %param.9) | copy-start | bytes 3145732
  7.2 59.2 %all-gather.3.cloned.1.call-start = ((), (), s32[]{:S(2)}) async-start(), calls=%async_computation | async-start | bytes 5013504 | tf_op jit(solution)/shard_map/all_gather | solution.py:21
  9.0 112.1 %all-reduce.2.cloned.1.call-start = ((), (), s32[]{:S(2)}) async-start(), calls=%async_computation.1 | async-start | bytes 2359296 | tf_op jit(solution)/shard_map/psum | solution.py:27
  68.1 11.5 %copy-start.1 = (s32[2]{0:T(128)S(1)}, s32[2]{0:T(128)}, u32[]{:S(2)}) copy-start(s32[2]{0:T(128)} %param.12) | copy-start | bytes 28
  79.5 85.2 %all-gather.5.cloned.1.call-start = ((), (), s32[]{:S(2)}) async-start(), calls=%async_computation.2 | async-start | bytes 2228224 | tf_op jit(solution)/shard_map/all_gather | solution.py:33
  166.1 46.8 %copy-start.2 = (s32[2]{0:T(128)S(1)}, s32[2]{0:T(128)}, u32[]{:S(2)}) copy-start(s32[2]{0:T(128)} %param.13) | copy-start | bytes 28
Sparse Core Ops, SparseCore 0:
  10.3 56.0 all-gather.2
  79.7 41.4 all-reduce.1
  123.5 41.1 all-gather.4
where the time goes:
time: 220 us
  waiting for transfers between devices  133 us (60%)
  blocking collectives  39.7 us (18%)
  matrix products  18.4 us (8%)
  between operations  13.8 us (6%)
  other arithmetic  12.3 us (6%)
  local copies, waits for them, and re-layouts  3.11 us (1%)
    all_gather x1, waiting for transfers between devices, local(): joined = lax.all_gather(joined, 'reader', axis=0, tiled=True)  57.3 us
    psum x1, blocking collectives, local(): scores = lax.psum(partial, ('owner', 'reader'))  39.7 us
    psum x1, waiting for transfers between devices, local(): whole = lax.psum(part, 'owner')  39.7 us
    all_gather x1, waiting for transfers between devices, local(): rot_a_all = lax.all_gather(rot_a_block, 'reader', axis=1, tiled=True)  35.5 us
    dot_general x1, matrix products, local(): jnp.einsum('tk,jk->tj', all_g, basis_g, preferred_element_type=jnp.float32)  10.2 us
    dot_general x1, matrix products, local(): jnp.einsum('stm,smn->stn', g_rows, scaled, preferred_element_type=jnp.flo...  6.41 us
    convert_element_type x1, other arithmetic, local(): denom = eigvals.astype(jnp.float32)  5.94 us
  transfers between devices with their start and end apart: 3, of which 3 were waited for; matrix products, arithmetic and copies ran while one was open for 4% of the time, Pallas kernels for 0%

commit v1 on v0

--- a/solution.py
+++ b/solution.py
@@ -4,6 +4,29 @@
 from jax.sharding import PartitionSpec as P
 
 SEQ = 128
+
+
+def joined_along(tiles, dim):
+    tiles = jnp.moveaxis(tiles, 0, dim)
+    lengths = tiles.shape
+    return tiles.reshape(*lengths[:dim], lengths[dim] * lengths[dim + 1], *lengths[dim + 2 :])
+
+
+def grow_blocks(x, axis):
+    size, place = (lax.axis_size(axis), lax.axis_index(axis))
+    blocks, bit = (x[None], 1)
+    while bit < size:
+        received = lax.ppermute(blocks, axis, [(i, i ^ bit) for i in range(size)])
+        low = place & bit == 0
+        blocks = jnp.concatenate(
+            [jnp.where(low, blocks, received), jnp.where(low, received, blocks)]
+        )
+        bit *= 2
+    return blocks
+
+
+def collect(array, axis, dim):
+    return joined_along(grow_blocks(array, axis), dim)
 
 
 def local(acts, grads, basis_a, basis_g, eigvals, lengths, shuffle):
@@ -18,7 +41,7 @@
     dim_ff = m_block * readers
     dim_d = width * owners
     joined = jnp.concatenate([grads, acts], axis=1)
-    joined = lax.all_gather(joined, "reader", axis=0, tiled=True)
+    joined = collect(joined, "reader", 0)
     all_g = joined[:, : grads.shape[1]]
     all_a = joined[:, grads.shape[1] :]
     part_g = jnp.einsum("tk,jk->tj", all_g, basis_g, preferred_element_type=jnp.float32)

time: 220 us -> 318 us (1.45)
  waiting for transfers between devices: 133 us -> 219 us
  starting transfers between devices: 0.12 us -> 7.84 us
  other arithmetic: 12.3 us -> 18.6 us
  matrix products: 18.4 us -> 14.1 us
    ppermute x0 -> x4, waiting for transfers between devices: none -> 142 us  [grow_blocks(): received = lax.ppermute(blocks, axis, [(i, i ^ bit) for i in range(size)])]
    all_gather x1 -> x0, waiting for transfers between devices: 57.3 us -> none  [local(): joined = lax.all_gather(joined, 'reader', axis=0, tiled=True)]
    ppermute x0 -> x4, starting transfers between devices: none -> 7.76 us  [grow_blocks(): received = lax.ppermute(blocks, axis, [(i, i ^ bit) for i in range(size)])]
    select_n x0 -> x4, other arithmetic: none -> 4.88 us  [grow_blocks(): jnp.where(low, blocks, received)]
  transfers between devices with their start and end apart: 3 -> 6, of which waited for: 3 -> 6; matrix products, arithmetic and copies ran while one was open for 4% -> 2% of each run, Pallas kernels for 0% -> 0%
where the time goes in v1:
time: 318 us
  waiting for transfers between devices  219 us (69%)
  blocking collectives  39.7 us (12%)
  other arithmetic  18.6 us (6%)
  between operations  14.2 us (4%)
  matrix products  14.1 us (4%)
  starting transfers between devices  7.84 us (2%)
  local copies, waits for them, and re-layouts  4.05 us (1%)
    ppermute x4, waiting for transfers between devices, grow_blocks(): received = lax.ppermute(blocks, axis, [(i, i ^ bit) for i in range(size)])  142 us
    psum x1, waiting for transfers between devices, local(): whole = lax.psum(part, 'owner')  41.8 us
    psum x1, blocking collectives, local(): scores = lax.psum(partial, ('owner', 'reader'))  39.7 us
    all_gather x1, waiting for transfers between devices, local(): rot_a_all = lax.all_gather(rot_a_block, 'reader', axis=1, tiled=True)  35.6 us
    ppermute x4, starting transfers between devices, grow_blocks(): received = lax.ppermute(blocks, axis, [(i, i ^ bit) for i in range(size)])  7.76 us
    dot_general x1, matrix products, local(): jnp.einsum('tk,jk->tj', all_g, basis_g, preferred_element_type=jnp.float32)  7.19 us
    dot_general x1, matrix products, local(): jnp.einsum('stm,smn->stn', g_rows, scaled, preferred_element_type=jnp.flo...  6.41 us
  transfers between devices with their start and end apart: 6, of which 6 were waited for; matrix products, arithmetic and copies ran while one was open for 2% of the time, Pallas kernels for 0%

profile of v1, /device:TPU:0, one launch (start us, length us, event | category | flops | bytes accessed | tf_op | source)
XLA Modules:
  0.0 317.6 jit_solution(14576028297786686182)
XLA Ops:
  7.2 0.0 copy-start
  7.2 0.0 all-reduce.2.cloned.1.call-start
  7.2 1.1 maximum_bitcast_fusion
  8.3 0.5 collective-permute-start
  8.8 1.2 collective-permute-done
  10.0 1.1 broadcast_select_fusion.7
  11.1 0.1 pad_maximum_fusion.4
  11.2 3.0 collective-permute-start.1
  14.1 13.6 %collective-permute-done.1 = bf16[2,16,9216]{2,1,0:T(8,128)(2,1)S(1)} collective-permute-done((bf16[2,16,9216]{2,1,0:T(8,128)(2,1)S(1)}, bf16[2,16,9216]{2,1,0:T(8,128)(2,1)S(1)}, u32[]{:S(2)}, u32[]{:S(2)}) %collective-permute-start.1) | collective-permute-done | bytes 589856 | tf_op jit(solution)/shard_map/ppermute | solution.py:19
  27.8 0.1 broadcast_select_fusion.5
  27.8 0.0 copy-start.1
  27.8 0.0 copy-start.2
  27.9 0.8 copy-done.1
  28.7 0.1 pad_maximum_fusion.2
  28.8 0.1 copy-done.2
  28.9 1.8 collective-permute-start.2
  30.7 25.8 %collective-permute-done.2 = bf16[4,16,9216]{2,1,0:T(8,128)(2,1)} collective-permute-done((bf16[4,16,9216]{2,1,0:T(8,128)(2,1)S(1)}, bf16[4,16,9216]{2,1,0:T(8,128)(2,1)}, u32[]{:S(2)}, u32[]{:S(2)}) %collective-permute-start.2) | collective-permute-done | bytes 1179680 | tf_op jit(solution)/shard_map/ppermute | solution.py:19
  56.5 1.8 broadcast_select_fusion.3
  58.3 1.6 pad_maximum_fusion.1
  59.9 2.5 collective-permute-start.3
  62.4 101.2 %collective-permute-done.3 = bf16[8,16,9216]{2,1,0:T(8,128)(2,1)} collective-permute-done((bf16[8,16,9216]{2,1,0:T(8,128)(2,1)}, bf16[8,16,9216]{2,1,0:T(8,128)(2,1)}, u32[]{:S(2)}, u32[]{:S(2)}) %collective-permute-start.3) | collective-permute-done | bytes 2359328 | tf_op jit(solution)/shard_map/ppermute | solution.py:19
  163.5 2.0 broadcast_select_fusion.1
  165.5 0.4 pad_maximum_fusion
  165.9 7.2 %fusion.3 = f32[256,896]{1,0:T(8,128)S(1)} fusion(bf16[896,7168]{1,0:T(8,128)(2,1)} %param.10, bf16[256,9216]{1,0:T(8,128)(2,1)S(1)} %bitcast.19), kind=kOutput, calls=%fused_computation.4 | convolution fusion | flops 3288334336 | bytes 17432576 | tf_op jit(solution)/shard_map/tk,jk->tj/dot_general | solution.py:47
  173.1 0.0 copy-done
  173.1 0.5 fusion.7
  173.6 0.0 copy-start.3
  173.6 1.1 pad_maximum_fusion.3
  174.7 0.0 all-reduce.2.cloned.1.call-update
  174.8 0.0 all-gather.2.cloned.1.call-start
  174.8 0.0 copy-done.3
  174.8 0.6 fusion.10
  175.4 1.3 compare_select_fusion.1
  176.7 41.8 %all-reduce.2.cloned.1.call-done = f32[256,1152]{1,0:T(8,128)} async-done(((f32[256,1152]{1,0:T(8,128)}), f32[256,1152]{1,0:T(8,128)}) %all-reduce.2.cloned.1.call-update) | async-done | bytes 1179664 | tf_op jit(solution)/shard_map/psum | solution.py:50
  218.5 1.4 multiply_convert_fusion
  219.9 0.7 slice.22
  220.6 0.0 all-gather.2.cloned.1.call-update
  220.6 5.9 %convert_element_type.22 = f32[896,2048]{1,0:T(8,128)} convert(bf16[896,2048]{1,0:T(8,128)(2,1)} %param.11) | non-fusion elementwise | flops 1835008 | bytes 11010048 | tf_op jit(solution)/shard_map/convert_element_type | solution.py:58
  226.6 35.6 %all-gather.2.cloned.1.call-done = bf16[256,4096]{1,0:T(8,128)(2,1)} async-done(((bf16[256,256]{1,0:T(8,128)(2,1)}), bf16[256,4096]{1,0:T(8,128)(2,1)}) %all-gather.2.cloned.1.call-update) | async-done | bytes 2097168 | tf_op jit(solution)/shard_map/all_gather | solution.py:56
  262.1 1.3 constant_dynamic-slice_fusion
  263.4 0.0 copy-start.4
  263.4 6.4 %fusion.6 = f32[2,128]{1,0:T(2,128)S(1)} fusion(bf16[2,128,2048]{2,1,0:T(8,128)(2,1)S(1)} %bitcast.21, bf16[2,128,896]{2,1,0:T(8,128)(2,1)S(1)} %bitcast.22, f32[896,2048]{1,0:T(8,128)} %convert_element_type.22), kind=kOutput, calls=%fused_computation.10 | convolution fusion | flops 1887960832 | bytes 8848384 | tf_op jit(solution)/shard_map/stm,smn->stn/dot_general | solution.py:63
  269.9 39.7 %psum.15 = f32[2,128]{1,0:T(2,128)S(1)} all-reduce(f32[2,128]{1,0:T(2,128)S(1)} %broadcast_multiply_fusion), channel_id=1, replica_groups=mesh['owner'=2,'reader'=16] {'owner','reader'}, use_global_device_ids=true, to_apply=%region_2.3 | all-reduce | flops 256 | bytes 2048 | tf_op jit(solution)/shard_map/psum | solution.py:65
  309.6 0.5 dynamic-slice_bitcast_fusion
  310.1 0.1 reduce_sum.28
  310.2 0.0 copy-done.4
  310.2 0.6 fusion.9
  (4 shorter events, 0.1 us)
Async XLA Ops:
  7.2 166.0 %copy-start = (bf16[256,2048]{1,0:T(8,128)(2,1)S(1)}, bf16[256,2048]{1,0:T(8,128)(2,1)}, u32[]{:S(2)}) copy-start(bf16[256,2048]{1,0:T(8,128)(2,1)} %param.9) | copy-start | bytes 3145732
  7.2 211.3 %all-reduce.2.cloned.1.call-start = ((), (), s32[]{:S(2)}) async-start(), calls=%async_computation | async-start | bytes 2359296 | tf_op jit(solution)/shard_map/psum | solution.py:50
  8.3 1.7 collective-permute-start
  11.2 16.6 %collective-permute-start.1 = (bf16[2,16,9216]{2,1,0:T(8,128)(2,1)S(1)}, bf16[2,16,9216]{2,1,0:T(8,128)(2,1)S(1)}, u32[]{:S(2)}, u32[]{:S(2)}) collective-permute-start(bf16[2,16,9216]{2,1,0:T(8,128)(2,1)S(1)} %pad_maximum_fusion.4), channel_id=1, source_target_pairs={{0,2},{1,3},{2,0},{3,1},{4,6},{5,7},{6,4},{7,5},{8,10},{9,11},{10,... | collective-permute-start | bytes 1769480 | tf_op jit(solution)/shard_map/ppermute | solution.py:19
  27.8 0.8 copy-start.1
  27.8 1.0 copy-start.2
  28.9 27.6 %collective-permute-start.2 = (bf16[4,16,9216]{2,1,0:T(8,128)(2,1)S(1)}, bf16[4,16,9216]{2,1,0:T(8,128)(2,1)}, u32[]{:S(2)}, u32[]{:S(2)}) collective-permute-start(bf16[4,16,9216]{2,1,0:T(8,128)(2,1)S(1)} %pad_maximum_fusion.2), channel_id=1, source_target_pairs={{0,4},{1,5},{2,6},{3,7},{4,0},{5,1},{6,2},{7,3},{8,12},{9,13},{10,... | collective-permute-start | bytes 3538952 | tf_op jit(solution)/shard_map/ppermute | solution.py:19
  59.9 103.7 %collective-permute-start.3 = (bf16[8,16,9216]{2,1,0:T(8,128)(2,1)}, bf16[8,16,9216]{2,1,0:T(8,128)(2,1)}, u32[]{:S(2)}, u32[]{:S(2)}) collective-permute-start(bf16[8,16,9216]{2,1,0:T(8,128)(2,1)} %pad_maximum_fusion.1), channel_id=1, source_target_pairs={{0,8},{1,9},{2,10},{3,11},{4,12},{5,13},{6,14},{7,15},{8,0},{9,1},... | collective-permute-start | bytes 7077896 | tf_op jit(solution)/shard_map/ppermute | solution.py:19
  173.6 1.2 copy-start.3
  174.8 87.4 %all-gather.2.cloned.1.call-start = ((), (), s32[]{:S(2)}) async-start(), calls=%async_computation.1 | async-start | bytes 2228224 | tf_op jit(solution)/shard_map/all_gather | solution.py:56
  263.4 46.8 %copy-start.4 = (s32[2]{0:T(128)S(1)}, s32[2]{0:T(128)}, u32[]{:S(2)}) copy-start(s32[2]{0:T(128)} %param.13) | copy-start | bytes 28
Sparse Core Ops, SparseCore 0:
  174.9 43.5 all-reduce.1
  220.9 41.1 all-gather.1

commit v2 on v0

--- a/solution.py
+++ b/solution.py
@@ -24,7 +24,7 @@
     part_g = jnp.einsum("tk,jk->tj", all_g, basis_g, preferred_element_type=jnp.float32)
     part_a = jnp.einsum("tk,jk->tj", all_a, basis_a, preferred_element_type=jnp.float32)
     part = jnp.concatenate([part_g, part_a], axis=1)
-    whole = lax.psum(part, "owner")
+    whole = jnp.sum(lax.all_gather(part, "owner"), axis=0)
     token = jnp.arange(rows, dtype=jnp.int32)
     live = (token % SEQ < lengths[token // SEQ]).astype(jnp.float32)
     rot = (whole * live[:, None]).astype(jnp.bfloat16)

time: 220 us -> 214 us (0.973)
  waiting for transfers between devices: 133 us -> 126 us
    psum x1 -> x0, waiting for transfers between devices: 39.7 us -> none  [local(): whole = lax.psum(part, 'owner')]
    all_gather x0 -> x1, waiting for transfers between devices: none -> 32.8 us  [local(): whole = jnp.sum(lax.all_gather(part, 'owner'), axis=0)]
where the time goes in v2:
time: 214 us
  waiting for transfers between devices  126 us (59%)
  blocking collectives  39.7 us (19%)
  matrix products  18.4 us (9%)
  between operations  13.8 us (6%)
  other arithmetic  12.9 us (6%)
  local copies, waits for them, and re-layouts  3.11 us (1%)
    all_gather x1, waiting for transfers between devices, local(): joined = lax.all_gather(joined, 'reader', axis=0, tiled=True)  57.3 us
    psum x1, blocking collectives, local(): scores = lax.psum(partial, ('owner', 'reader'))  39.7 us
    all_gather x1, waiting for transfers between devices, local(): rot_a_all = lax.all_gather(rot_a_block, 'reader', axis=1, tiled=True)  35.4 us
    all_gather x1, waiting for transfers between devices, local(): whole = jnp.sum(lax.all_gather(part, 'owner'), axis=0)  32.8 us
    dot_general x1, matrix products, local(): jnp.einsum('tk,jk->tj', all_g, basis_g, preferred_element_type=jnp.float32)  10.2 us
    dot_general x1, matrix products, local(): jnp.einsum('stm,smn->stn', g_rows, scaled, preferred_element_type=jnp.flo...  6.41 us
    convert_element_type x1, other arithmetic, local(): denom = eigvals.astype(jnp.float32)  5.94 us
  transfers between devices with their start and end apart: 3, of which 3 were waited for; matrix products, arithmetic and copies ran while one was open for 4% of the time, Pallas kernels for 0%

profile of v2, /device:TPU:0, one launch (start us, length us, event | category | flops | bytes accessed | tf_op | source)
XLA Modules:
  0.0 213.6 jit_solution(15283375836024627101)
XLA Ops:
  7.2 0.0 copy-start
  7.2 0.0 all-gather.5.cloned.1.call-start
  7.2 1.8 pad_maximum_fusion.1
  9.0 0.0 all-gather.5.cloned.1.call-update
  9.0 0.0 all-gather.9.cloned.1.call-start
  9.1 57.3 %all-gather.5.cloned.1.call-done = bf16[256,9216]{1,0:T(8,128)(2,1)} async-done(((bf16[16,9216]{1,0:T(8,128)(2,1)}), bf16[256,9216]{1,0:T(8,128)(2,1)}) %all-gather.5.cloned.1.call-update) | async-done | bytes 4718608 | tf_op jit(solution)/shard_map/all_gather | solution.py:21
  66.4 0.0 copy-done
  66.4 1.7 fusion.7
  68.1 0.0 copy-start.1
  68.1 10.2 %fusion.3 = f32[256,896]{1,0:T(8,128)S(1)} fusion(bf16[896,7168]{1,0:T(8,128)(2,1)} %param.10, bf16[256,9216]{1,0:T(8,128)(2,1)} %all-gather.5.cloned.1.call-done), kind=kOutput, calls=%fused_computation.3 | convolution fusion | flops 3288334336 | bytes 17432576 | tf_op jit(solution)/shard_map/tk,jk->tj/dot_general | solution.py:24
  78.4 1.1 pad_maximum_fusion
  79.5 0.0 all-gather.9.cloned.1.call-update
  79.5 0.0 all-gather.7.cloned.1.call-start
  79.6 0.0 copy-done.1
  79.6 0.6 fusion.10
  80.2 1.3 compare_select_fusion.1
  81.5 32.8 %all-gather.9.cloned.1.call-done = f32[512,1152]{1,0:T(8,128)} async-done(((f32[256,1152]{1,0:T(8,128)}), f32[512,1152]{1,0:T(8,128)}) %all-gather.9.cloned.1.call-update) | async-done | bytes 2359312 | tf_op jit(solution)/shard_map/all_gather | solution.py:27
  114.3 1.9 reduce_sum.36
  116.2 0.1 multiply_convert_fusion
  116.4 0.7 slice.22
  117.0 0.0 all-gather.7.cloned.1.call-update
  117.1 5.9 %convert_element_type.22 = f32[896,2048]{1,0:T(8,128)} convert(bf16[896,2048]{1,0:T(8,128)(2,1)} %param.11) | non-fusion elementwise | flops 1835008 | bytes 11010048 | tf_op jit(solution)/shard_map/convert_element_type | solution.py:35
  123.0 35.4 %all-gather.7.cloned.1.call-done = bf16[256,4096]{1,0:T(8,128)(2,1)} async-done(((bf16[256,256]{1,0:T(8,128)(2,1)}), bf16[256,4096]{1,0:T(8,128)(2,1)}) %all-gather.7.cloned.1.call-update) | async-done | bytes 2097168 | tf_op jit(solution)/shard_map/all_gather | solution.py:33
  158.4 1.3 constant_dynamic-slice_fusion
  159.7 0.0 copy-start.2
  159.7 6.4 %fusion.6 = f32[2,128]{1,0:T(2,128)S(1)} fusion(bf16[2,128,2048]{2,1,0:T(8,128)(2,1)S(1)} %bitcast.14, bf16[2,128,896]{2,1,0:T(8,128)(2,1)S(1)} %bitcast.15, f32[896,2048]{1,0:T(8,128)} %convert_element_type.22), kind=kOutput, calls=%fused_computation.6 | convolution fusion | flops 1887960832 | bytes 8848384 | tf_op jit(solution)/shard_map/stm,smn->stn/dot_general | solution.py:40
  166.1 39.7 %psum.7 = f32[2,128]{1,0:T(2,128)S(1)} all-reduce(f32[2,128]{1,0:T(2,128)S(1)} %broadcast_multiply_fusion), channel_id=1, replica_groups=mesh['owner'=2,'reader'=16] {'owner','reader'}, use_global_device_ids=true, to_apply=%region_2.3 | all-reduce | flops 256 | bytes 2048 | tf_op jit(solution)/shard_map/psum | solution.py:42
  205.8 0.1 reduce_sum.38
  206.0 0.5 dynamic-slice_bitcast_fusion
  206.5 0.0 copy-done.2
  206.5 0.6 fusion.9
  (4 shorter events, 0.1 us)
Async XLA Ops:
  7.2 59.3 %copy-start = (bf16[256,2048]{1,0:T(8,128)(2,1)S(1)}, bf16[256,2048]{1,0:T(8,128)(2,1)}, u32[]{:S(2)}) copy-start(bf16[256,2048]{1,0:T(8,128)(2,1)} %param.9) | copy-start | bytes 3145732
  7.2 59.2 %all-gather.5.cloned.1.call-start = ((), (), s32[]{:S(2)}) async-start(), calls=%async_computation | async-start | bytes 5013504 | tf_op jit(solution)/shard_map/all_gather | solution.py:21
  9.0 105.3 %all-gather.9.cloned.1.call-start = ((), (), s32[]{:S(2)}) async-start(), calls=%async_computation.2 | async-start | bytes 3538944 | tf_op jit(solution)/shard_map/all_gather | solution.py:27
  68.1 11.4 %copy-start.1 = (s32[2]{0:T(128)S(1)}, s32[2]{0:T(128)}, u32[]{:S(2)}) copy-start(s32[2]{0:T(128)} %param.12) | copy-start | bytes 28
  79.5 78.9 %all-gather.7.cloned.1.call-start = ((), (), s32[]{:S(2)}) async-start(), calls=%async_computation.1 | async-start | bytes 2228224 | tf_op jit(solution)/shard_map/all_gather | solution.py:33
  159.7 46.8 %copy-start.2 = (s32[2]{0:T(128)S(1)}, s32[2]{0:T(128)}, u32[]{:S(2)}) copy-start(s32[2]{0:T(128)} %param.13) | copy-start | bytes 28
Sparse Core Ops, SparseCore 0:
  10.3 56.0 all-gather.4
  79.6 34.6 all-gather.8
  117.2 41.1 all-gather.6
